TPU v7x, 256 devices: a whole 4x4x8 slice. The times are simulated.
256 devices in a mesh: sta: 16 (over z, y_lo), win: 16 (over x, y_hi, core).
Axes of the slice: x: 4, y: 4 (y_hi: 2, y_lo: 2; y = y_hi * 2 + y_lo), z: 8, core: 2. Of those that a mesh axis runs over, the one named last changes fastest.
Arguments:
- spectra: bfloat16 [16, 1024, 4096], P('win', 'sta'), may hold values from -80 to 80
- pair_first: int32 [16, 9, 48], P('sta'), may hold values from 0 to 63
- pair_second: int32 [16, 9, 48], P('sta'), may hold values from 0 to 63
- pair_owner: int32 [16, 9, 48], P('sta'), may hold values from 0 to 15, as said below
Outputs:
- correlations: bfloat16 [16, 864, 1024], P('sta', 'win')
Inputs may be any that keep to these rules, and one draw needn't show every extreme that they name: `pair_owner`: in each block row at most 54 pairs share an owner, and one owner of the row has exactly 54.
All inputs are finite; a program needn't handle non-finite values.
Results may differ from a plain program's by a relative error of at most 0.014.
Values may be sent and summed in bfloat16 or wider, within the bound.
No kernel may reach another device: no remote copies, remote signals or barrier semaphores. Data moves between devices by JAX's collectives and lax.ppermute only.
A program may use at most 64 MiB of HBM per device.

v0:
```python
import math

import jax
import jax.numpy as jnp
from jax import lax
from jax.sharding import PartitionSpec as P

LAGS = 1024
SMOOTH_HALF = 10


floor_level = 0.5


def passed_along(value, axis, by):
    peers = lax.axis_size(axis)
    return lax.ppermute(value, axis, [(i, (i + by) % peers) for i in range(peers)])


def whiten(spectra, half_width):
    bin_count = spectra.shape[-1] // 2
    real_part = spectra[..., :bin_count].astype(jnp.float32)
    imag_part = spectra[..., bin_count:].astype(jnp.float32)
    amplitude = jnp.sqrt(real_part * real_part + imag_part * imag_part)
    padded = jnp.pad(amplitude, ((0, 0), (0, 0), (half_width, half_width)))
    running = padded[..., 0:bin_count]
    for offset in range(1, 2 * half_width + 1):
        running = running + padded[..., offset : offset + bin_count]
    smooth = running / (2 * half_width + 1)
    inverse = 1.0 / jnp.maximum(smooth, floor_level)
    return jnp.concatenate([real_part * inverse, imag_part * inverse], axis=-1).astype(jnp.bfloat16)


def cross_rows(own_block, other_block, first_index, second_index):
    bin_count = own_block.shape[-1] // 2
    left_rows = jnp.take(own_block, first_index, axis=1).astype(jnp.float32)
    right_rows = jnp.take(other_block, second_index, axis=1).astype(jnp.float32)
    left_real, left_imag = (left_rows[..., :bin_count], left_rows[..., bin_count:])
    right_real, right_imag = (right_rows[..., :bin_count], right_rows[..., bin_count:])
    real_cross = left_real * right_real + left_imag * right_imag
    imag_cross = left_imag * right_real - left_real * right_imag
    return jnp.sum(jnp.concatenate([real_cross, imag_cross], axis=-1), axis=0)


def owner_slots(owners, groups):
    flat_owner = owners.reshape(-1)
    owner_hits = (flat_owner[:, None] == jnp.arange(groups, dtype=jnp.int32)[None, :]).astype(
        jnp.int32
    )
    before = jnp.cumsum(owner_hits, axis=0) - owner_hits
    return (flat_owner, jnp.sum(before * owner_hits, axis=1))


def lag_table(bin_count, lag_count, row_start, rows):
    row_index = row_start + jnp.arange(rows, dtype=jnp.int32)
    frequency = row_index % bin_count
    lag_value = jnp.arange(lag_count, dtype=jnp.int32) - lag_count // 2
    phase_step = jnp.mod(frequency[:, None] * lag_value[None, :], 2 * bin_count)
    angle_value = phase_step.astype(jnp.float32) * (2.0 * math.pi / (2 * bin_count))
    weight = jnp.where(frequency == 0, 1.0, 2.0).astype(jnp.float32)[:, None]
    values = (
        jnp.where((row_index < bin_count)[:, None], jnp.cos(angle_value), -jnp.sin(angle_value))
        * weight
    )
    return values.astype(jnp.bfloat16)


def build_table(bin_count, lag_count):
    block_rows = min(1024, 2 * bin_count)
    blocks = [
        lag_table(bin_count, lag_count, start, block_rows)
        for start in range(0, 2 * bin_count, block_rows)
    ]
    return jnp.concatenate(blocks, axis=0)


def transform(stacked, table, factor):
    return (jnp.dot(stacked, table, preferred_element_type=jnp.float32) * factor).astype(
        jnp.bfloat16
    )


def local(spectra, pair_first, pair_second, pair_owner):
    groups = lax.axis_size("win")
    bin_count = spectra.shape[-1] // 2
    windows_all = spectra.shape[0] * groups
    factor = 1.0 / math.sqrt(2 * bin_count * windows_all)
    whitened = whiten(spectra, SMOOTH_HALF)
    first_rows = pair_first[0]
    second_rows = pair_second[0]
    offsets = first_rows.shape[0]
    pieces = [cross_rows(whitened, whitened, first_rows[0], second_rows[0]).astype(jnp.bfloat16)]
    cycle_block = whitened
    for offset_step in range(1, offsets):
        cycle_block = passed_along(cycle_block, "sta", -1)
        pieces.append(
            cross_rows(
                whitened, cycle_block, first_rows[offset_step], second_rows[offset_step]
            ).astype(jnp.bfloat16)
        )
    partial_value = jnp.concatenate(pieces, axis=0)
    pair_rows = partial_value.shape[0]
    capacity = 2 * pair_rows // groups
    owners, slot_of = owner_slots(pair_owner[0], groups)
    target = owners * capacity + slot_of
    table = build_table(bin_count, LAGS)
    outgoing = (
        jnp.zeros((groups * capacity, 2 * bin_count), jnp.bfloat16).at[target].set(partial_value)
    )
    outgoing = outgoing.reshape(groups, capacity, 2 * bin_count)
    stacked = jnp.sum(
        lax.all_to_all(outgoing, "win", split_axis=0, concat_axis=0, tiled=True).astype(
            jnp.float32
        ),
        axis=0,
    ).astype(jnp.bfloat16)
    result = transform(stacked, table, factor)
    return result[None]


def solution(mesh):
    placed = (
        P("win", "sta", None),
        P("sta", None, None),
        P("sta", None, None),
        P("sta", None, None),
    )
    return jax.shard_map(
        local, mesh=mesh, in_specs=placed, out_specs=P("sta", "win", None), check_vma=False
    )
```

profile of v0, /device:TPU:1, one launch (start us, length us, event | category | flops | bytes accessed | tf_op | source)
XLA Modules:
  0.0 279.4 jit_solution(13595314928810097222)
XLA Ops:
  0.0 1.3 fusion.32
  1.3 3.7 %fusion.33 = (bf16[1,64,2048]{2,1,0:T(8,128)(2,1)S(1)}, f32[1,64,2048]{2,1,0:T(8,128)S(1)}) fusion(bf16[1,64,4096]{2,1,0:T(8,128)(2,1)} %param.6, f32[1,64,2048]{2,1,0:T(8,128)S(1)} %fusion.32), kind=kLoop, calls=%fused_computation.74 | loop fusion | flops 3407872 | bytes 1572864 | tf_op jit(solution)/shard_map/convert.22
  5.0 1.0 fusion.34
  6.0 0.9 pad_maximum_fusion
  6.9 7.4 %collective-permute-start = (bf16[1,64,4096]{2,1,0:T(8,128)(2,1)}, bf16[1,64,4096]{2,1,0:T(8,128)(2,1)S(1)}, u32[]{:S(2)}, u32[]{:S(2)}) collective-permute-start(bf16[1,64,4096]{2,1,0:T(8,128)(2,1)} %get-tuple-element.64), channel_id=1, source_target_pairs={{0,240},{16,0},{32,16},{48,32},{64,48},{80,64},{96,80},{112,96},{1... | collective-permute-start | bytes 1572872 | tf_op jit(solution)/shard_map/ppermute | solution.py:17
  14.4 0.8 gather_fusion
  15.2 0.8 gather_fusion.1
  16.0 0.8 gather_fusion.2
  16.8 0.8 gather_fusion.4
  17.7 0.8 gather_fusion.6
  18.5 0.8 gather_fusion.8
  19.3 1.5 gather_fusion.10
  20.8 1.6 gather_fusion.12
  22.4 1.6 gather_fusion.14
  24.0 1.5 gather_fusion.16
  25.7 1.2 reduce-window.6
  27.5 1.0 fusion.67
  28.5 1.0 fusion.65
  29.6 1.0 fusion.63
  30.6 1.0 fusion.61
  31.6 1.0 fusion.59
  33.4 0.8 fusion.43
  34.2 1.5 gather_fusion.3
  35.8 10.0 %collective-permute-done.1 = bf16[1,64,4096]{2,1,0:T(8,128)(2,1)S(1)} collective-permute-done((bf16[1,64,4096]{2,1,0:T(8,128)(2,1)S(1)}, bf16[1,64,4096]{2,1,0:T(8,128)(2,1)S(1)}, u32[]{:S(2)}, u32[]{:S(2)}) %collective-permute-start.1) | collective-permute-done | bytes 524320 | tf_op jit(solution)/shard_map/ppermute | solution.py:17
  45.8 0.8 gather_fusion.5
  46.6 1.2 fusion.64
  47.8 2.4 collective-permute-start.2
  50.2 1.2 add_convert_fusion.7
  51.5 8.1 %collective-permute-done.2 = bf16[1,64,4096]{2,1,0:T(8,128)(2,1)S(1)} collective-permute-done((bf16[1,64,4096]{2,1,0:T(8,128)(2,1)S(1)}, bf16[1,64,4096]{2,1,0:T(8,128)(2,1)S(1)}, u32[]{:S(2)}, u32[]{:S(2)}) %collective-permute-start.2) | collective-permute-done | bytes 524320 | tf_op jit(solution)/shard_map/ppermute | solution.py:17
  59.7 4.3 %collective-permute-start.3 = (bf16[1,64,4096]{2,1,0:T(8,128)(2,1)S(1)}, bf16[1,64,4096]{2,1,0:T(8,128)(2,1)S(1)}, u32[]{:S(2)}, u32[]{:S(2)}) collective-permute-start(bf16[1,64,4096]{2,1,0:T(8,128)(2,1)S(1)} %collective-permute-done.2), channel_id=1, source_target_pairs={{0,240},{16,0},{32,16},{48,32},{64,48},{80,64},{96,80},{112,96},{1... | collective-permute-start | bytes 1572872 | tf_op jit(solution)/shard_map/ppermute | solution.py:17
  64.0 0.8 fusion.44
  64.7 0.8 fusion.45
  65.5 1.5 gather_fusion.7
  67.1 5.5 %collective-permute-done.3 = bf16[1,64,4096]{2,1,0:T(8,128)(2,1)S(1)} collective-permute-done((bf16[1,64,4096]{2,1,0:T(8,128)(2,1)S(1)}, bf16[1,64,4096]{2,1,0:T(8,128)(2,1)S(1)}, u32[]{:S(2)}, u32[]{:S(2)}) %collective-permute-start.3) | collective-permute-done | bytes 524320 | tf_op jit(solution)/shard_map/ppermute | solution.py:17
  72.6 0.8 gather_fusion.9
  73.4 1.2 fusion.60
  74.6 4.6 %collective-permute-start.4 = (bf16[1,64,4096]{2,1,0:T(8,128)(2,1)S(1)}, bf16[1,64,4096]{2,1,0:T(8,128)(2,1)S(1)}, u32[]{:S(2)}, u32[]{:S(2)}) collective-permute-start(bf16[1,64,4096]{2,1,0:T(8,128)(2,1)S(1)} %collective-permute-done.3), channel_id=1, source_target_pairs={{0,240},{16,0},{32,16},{48,32},{64,48},{80,64},{96,80},{112,96},{1... | collective-permute-start | bytes 1572872 | tf_op jit(solution)/shard_map/ppermute | solution.py:17
  79.2 1.2 add_convert_fusion.5
  80.5 6.4 %collective-permute-done.4 = bf16[1,64,4096]{2,1,0:T(8,128)(2,1)S(1)} collective-permute-done((bf16[1,64,4096]{2,1,0:T(8,128)(2,1)S(1)}, bf16[1,64,4096]{2,1,0:T(8,128)(2,1)S(1)}, u32[]{:S(2)}, u32[]{:S(2)}) %collective-permute-start.4) | collective-permute-done | bytes 524320 | tf_op jit(solution)/shard_map/ppermute | solution.py:17
  87.0 4.3 %collective-permute-start.5 = (bf16[1,64,4096]{2,1,0:T(8,128)(2,1)S(1)}, bf16[1,64,4096]{2,1,0:T(8,128)(2,1)S(1)}, u32[]{:S(2)}, u32[]{:S(2)}) collective-permute-start(bf16[1,64,4096]{2,1,0:T(8,128)(2,1)S(1)} %collective-permute-done.4), channel_id=1, source_target_pairs={{0,240},{16,0},{32,16},{48,32},{64,48},{80,64},{96,80},{112,96},{1... | collective-permute-start | bytes 1572872 | tf_op jit(solution)/shard_map/ppermute | solution.py:17
  91.3 0.8 fusion.46
  92.1 0.8 fusion.47
  92.9 1.5 gather_fusion.11
  94.4 3.8 %collective-permute-done.5 = bf16[1,64,4096]{2,1,0:T(8,128)(2,1)S(1)} collective-permute-done((bf16[1,64,4096]{2,1,0:T(8,128)(2,1)S(1)}, bf16[1,64,4096]{2,1,0:T(8,128)(2,1)S(1)}, u32[]{:S(2)}, u32[]{:S(2)}) %collective-permute-start.5) | collective-permute-done | bytes 524320 | tf_op jit(solution)/shard_map/ppermute | solution.py:17
  98.2 0.8 gather_fusion.13
  99.0 1.2 fusion.56
  100.2 4.4 %collective-permute-start.6 = (bf16[1,64,4096]{2,1,0:T(8,128)(2,1)S(1)}, bf16[1,64,4096]{2,1,0:T(8,128)(2,1)S(1)}, u32[]{:S(2)}, u32[]{:S(2)}) collective-permute-start(bf16[1,64,4096]{2,1,0:T(8,128)(2,1)S(1)} %collective-permute-done.5), channel_id=1, source_target_pairs={{0,240},{16,0},{32,16},{48,32},{64,48},{80,64},{96,80},{112,96},{1... | collective-permute-start | bytes 1572872 | tf_op jit(solution)/shard_map/ppermute | solution.py:17
  104.5 1.2 add_convert_fusion.3
  105.9 4.8 %collective-permute-done.6 = bf16[1,64,4096]{2,1,0:T(8,128)(2,1)S(1)} collective-permute-done((bf16[1,64,4096]{2,1,0:T(8,128)(2,1)S(1)}, bf16[1,64,4096]{2,1,0:T(8,128)(2,1)S(1)}, u32[]{:S(2)}, u32[]{:S(2)}) %collective-permute-start.6) | collective-permute-done | bytes 524320 | tf_op jit(solution)/shard_map/ppermute | solution.py:17
  110.7 4.0 %collective-permute-start.7 = (bf16[1,64,4096]{2,1,0:T(8,128)(2,1)S(1)}, bf16[1,64,4096]{2,1,0:T(8,128)(2,1)S(1)}, u32[]{:S(2)}, u32[]{:S(2)}) collective-permute-start(bf16[1,64,4096]{2,1,0:T(8,128)(2,1)S(1)} %collective-permute-done.6), channel_id=1, source_target_pairs={{0,240},{16,0},{32,16},{48,32},{64,48},{80,64},{96,80},{112,96},{1... | collective-permute-start | bytes 1572872 | tf_op jit(solution)/shard_map/ppermute | solution.py:17
  114.7 0.8 fusion.48
  115.5 0.8 fusion.49
  116.2 0.8 gather_fusion.15
  117.0 4.9 %collective-permute-done.7 = bf16[1,64,4096]{2,1,0:T(8,128)(2,1)S(1)} collective-permute-done((bf16[1,64,4096]{2,1,0:T(8,128)(2,1)S(1)}, bf16[1,64,4096]{2,1,0:T(8,128)(2,1)S(1)}, u32[]{:S(2)}, u32[]{:S(2)}) %collective-permute-start.7) | collective-permute-done | bytes 524320 | tf_op jit(solution)/shard_map/ppermute | solution.py:17
  122.0 0.8 gather_fusion.17
  123.2 0.8 fusion.50
  123.9 0.8 fusion.51
  124.7 10.9 %scatter_custom_fusion = bf16[864,4096]{1,0:T(8,128)(2,1)} fusion(s32[432]{0:T(512)S(1)} %bitcast.207, bf16[432,4096]{1,0:T(8,128)(2,1)} %fusion.51, bf16[]{:T(256)} %constant.92.clone.1), kind=kCustom, calls=%fused_computation.63 | custom fusion | bytes 7078400 | tf_op jit(solution)/shard_map/scatter | solution.py:108
  135.6 7.1 %reshape.244 = bf16[16,54,4096]{2,1,0:T(8,128)(2,1)} reshape(bf16[864,4096]{1,0:T(8,128)(2,1)} %scatter_custom_fusion) | data formatting | bytes 14155776 | tf_op jit(solution)/shard_map/reshape | solution.py:110
  142.6 14.2 %all-to-all-start = ((bf16[16,54,4096]{2,1,0:T(8,128)(2,1)}), bf16[16,54,4096]{2,1,0:T(8,128)(2,1)}, u32[]{:S(2)}, u32[]{:S(2)}) async-start(bf16[16,54,4096]{2,1,0:T(8,128)(2,1)} %reshape.244), calls=%async_computation | async-start | bytes 14680064 | tf_op jit(solution)/shard_map/all_to_all | solution.py:112
  156.9 71.0 %multiply_convert_fusion.3 = (bf16[1024,1024]{1,0:T(8,128)(2,1)S(1)}, bf16[1024,1024]{1,0:T(8,128)(2,1)}, bf16[1024,1024]{1,0:T(8,128)(2,1)}, bf16[1024,1024]{1,0:T(8,128)(2,1)}) fusion(f32[1024]{0:T(1024)S(1)} %get-tuple-element.131, s32[1024]{0:T(1024)S(1)} %iota_add_fusion.3, s32[1024]{0:T(1024)S(1)} %get-tuple-element.123, ...), kind=kLoop, calls=%fused_computation.62 | loop fusion | flops 75497472 | bytes 8429568 | tf_op jit(solution)/shard_map/convert_element_type | solution.py:65
  227.9 42.8 %all-to-all-done = bf16[16,54,4096]{2,1,0:T(8,128)(2,1)} async-done(((bf16[16,54,4096]{2,1,0:T(8,128)(2,1)}), bf16[16,54,4096]{2,1,0:T(8,128)(2,1)}, u32[]{:S(2)}, u32[]{:S(2)}) %all-to-all-start) | async-done | bytes 7077920 | tf_op jit(solution)/shard_map/all_to_all | solution.py:112
  270.7 4.5 %reduce_sum.29 = bf16[54,4096]{1,0:T(8,128)(2,1)S(1)} reduce(bf16[16,54,4096]{2,1,0:T(8,128)(2,1)} %all-to-all-done, bf16[]{:T(256)} %constant.92.clone.1), dimensions={0}, to_apply=%region_4.6 | reduce | flops 3317760 | bytes 7520258 | tf_op jit(solution)/shard_map/reduce_sum | solution.py:111
  275.2 4.3 %fusion.28 = bf16[1,54,1024]{2,1,0:T(8,128)(2,1)} fusion(bf16[54,4096]{1,0:T(8,128)(2,1)S(1)} %reduce_sum.29, bf16[1024,1024]{1,0:T(8,128)(2,1)} %get-tuple-element.101, bf16[1024,1024]{1,0:T(8,128)(2,1)} %get-tuple-element.100, bf16[1024,1024]{1,0:T(8,128)(2,1)} %get-tuple-element.99, bf16[1024,1024]{1,0:T(8,128)(2,1)S(1)} %get-tuple-element.98), kind=kOutput, calls=%fused_computation.67 | convolution fusion | flops 486649856 | bytes 8941568 | tf_op jit(solution)/shard_map/dot_general | solution.py:78
  (65 shorter events, 2.4 us)
Async XLA Ops:
  0.0 14.3 %copy-start.6 = (s32[1,9,48]{2,0,1:T(1,128)S(1)}, s32[1,9,48]{2,0,1:T(1,128)}, u32[]{:S(2)}) copy-start(s32[1,9,48]{2,0,1:T(1,128)} %param.7) | copy-start | bytes 5188
  0.0 14.4 %copy-start.7 = (s32[1,9,48]{2,0,1:T(1,128)S(1)}, s32[1,9,48]{2,0,1:T(1,128)}, u32[]{:S(2)}) copy-start(s32[1,9,48]{2,0,1:T(1,128)} %param.8) | copy-start | bytes 5188
  6.9 26.3 %collective-permute-start = (bf16[1,64,4096]{2,1,0:T(8,128)(2,1)}, bf16[1,64,4096]{2,1,0:T(8,128)(2,1)S(1)}, u32[]{:S(2)}, u32[]{:S(2)}) collective-permute-start(bf16[1,64,4096]{2,1,0:T(8,128)(2,1)} %get-tuple-element.64), channel_id=1, source_target_pairs={{0,240},{16,0},{32,16},{48,32},{64,48},{80,64},{96,80},{112,96},{1... | collective-permute-start | bytes 1572872 | tf_op jit(solution)/shard_map/ppermute | solution.py:17
  22.4 3.1 %copy-start.8 = (s32[1,9,48]{2,0,1:T(1,128)S(1)}, s32[1,9,48]{2,0,1:T(1,128)}, u32[]{:S(2)}) copy-start(s32[1,9,48]{2,0,1:T(1,128)} %param.9) | copy-start | bytes 5188
  25.5 6.1 %copy-start.2 = (bf16[48,4096]{1,0:T(8,128)(2,1)S(1)}, bf16[48,4096]{1,0:T(8,128)(2,1)}, u32[]{:S(2)}) copy-start(bf16[48,4096]{1,0:T(8,128)(2,1)} %gather_fusion.10) | copy-start | bytes 1179652
  27.3 5.4 %copy-start.3 = (bf16[48,4096]{1,0:T(8,128)(2,1)S(1)}, bf16[48,4096]{1,0:T(8,128)(2,1)}, u32[]{:S(2)}) copy-start(bf16[48,4096]{1,0:T(8,128)(2,1)} %gather_fusion.12) | copy-start | bytes 1179652
  27.4 5.4 %copy-start.5 = (bf16[48,4096]{1,0:T(8,128)(2,1)S(1)}, bf16[48,4096]{1,0:T(8,128)(2,1)}, u32[]{:S(2)}) copy-start(bf16[48,4096]{1,0:T(8,128)(2,1)} %gather_fusion.14) | copy-start | bytes 1179652
  27.5 5.4 %copy-start.4 = (bf16[48,4096]{1,0:T(8,128)(2,1)S(1)}, bf16[48,4096]{1,0:T(8,128)(2,1)}, u32[]{:S(2)}) copy-start(bf16[48,4096]{1,0:T(8,128)(2,1)} %gather_fusion.16) | copy-start | bytes 1179652
  33.2 12.6 %collective-permute-start.1 = (bf16[1,64,4096]{2,1,0:T(8,128)(2,1)S(1)}, bf16[1,64,4096]{2,1,0:T(8,128)(2,1)S(1)}, u32[]{:S(2)}, u32[]{:S(2)}) collective-permute-start(bf16[1,64,4096]{2,1,0:T(8,128)(2,1)S(1)} %collective-permute-done), channel_id=1, source_target_pairs={{0,240},{16,0},{32,16},{48,32},{64,48},{80,64},{96,80},{112,96},{1... | collective-permute-start | bytes 1572872 | tf_op jit(solution)/shard_map/ppermute | solution.py:17
  46.6 4.8 %copy-start.1 = (f32[1,48,4096]{2,1,0:T(8,128)S(1)}, f32[1,48,4096]{2,1,0:T(8,128)}, u32[]{:S(2)}) copy-start(f32[1,48,4096]{2,1,0:T(8,128)} %fusion.65) | copy-start | bytes 2359300
  47.8 11.8 %collective-permute-start.2 = (bf16[1,64,4096]{2,1,0:T(8,128)(2,1)S(1)}, bf16[1,64,4096]{2,1,0:T(8,128)(2,1)S(1)}, u32[]{:S(2)}, u32[]{:S(2)}) collective-permute-start(bf16[1,64,4096]{2,1,0:T(8,128)(2,1)S(1)} %collective-permute-done.1), channel_id=1, source_target_pairs={{0,240},{16,0},{32,16},{48,32},{64,48},{80,64},{96,80},{112,96},{1... | collective-permute-start | bytes 1572872 | tf_op jit(solution)/shard_map/ppermute | solution.py:17
  59.7 12.9 %collective-permute-start.3 = (bf16[1,64,4096]{2,1,0:T(8,128)(2,1)S(1)}, bf16[1,64,4096]{2,1,0:T(8,128)(2,1)S(1)}, u32[]{:S(2)}, u32[]{:S(2)}) collective-permute-start(bf16[1,64,4096]{2,1,0:T(8,128)(2,1)S(1)} %collective-permute-done.2), channel_id=1, source_target_pairs={{0,240},{16,0},{32,16},{48,32},{64,48},{80,64},{96,80},{112,96},{1... | collective-permute-start | bytes 1572872 | tf_op jit(solution)/shard_map/ppermute | solution.py:17
  73.4 7.0 %copy-start = (f32[1,48,4096]{2,1,0:T(8,128)S(1)}, f32[1,48,4096]{2,1,0:T(8,128)}, u32[]{:S(2)}) copy-start(f32[1,48,4096]{2,1,0:T(8,128)} %fusion.61) | copy-start | bytes 2359300
  74.6 12.3 %collective-permute-start.4 = (bf16[1,64,4096]{2,1,0:T(8,128)(2,1)S(1)}, bf16[1,64,4096]{2,1,0:T(8,128)(2,1)S(1)}, u32[]{:S(2)}, u32[]{:S(2)}) collective-permute-start(bf16[1,64,4096]{2,1,0:T(8,128)(2,1)S(1)} %collective-permute-done.3), channel_id=1, source_target_pairs={{0,240},{16,0},{32,16},{48,32},{64,48},{80,64},{96,80},{112,96},{1... | collective-permute-start | bytes 1572872 | tf_op jit(solution)/shard_map/ppermute | solution.py:17
  87.0 11.2 %collective-permute-start.5 = (bf16[1,64,4096]{2,1,0:T(8,128)(2,1)S(1)}, bf16[1,64,4096]{2,1,0:T(8,128)(2,1)S(1)}, u32[]{:S(2)}, u32[]{:S(2)}) collective-permute-start(bf16[1,64,4096]{2,1,0:T(8,128)(2,1)S(1)} %collective-permute-done.4), channel_id=1, source_target_pairs={{0,240},{16,0},{32,16},{48,32},{64,48},{80,64},{96,80},{112,96},{1... | collective-permute-start | bytes 1572872 | tf_op jit(solution)/shard_map/ppermute | solution.py:17
  100.2 10.5 %collective-permute-start.6 = (bf16[1,64,4096]{2,1,0:T(8,128)(2,1)S(1)}, bf16[1,64,4096]{2,1,0:T(8,128)(2,1)S(1)}, u32[]{:S(2)}, u32[]{:S(2)}) collective-permute-start(bf16[1,64,4096]{2,1,0:T(8,128)(2,1)S(1)} %collective-permute-done.5), channel_id=1, source_target_pairs={{0,240},{16,0},{32,16},{48,32},{64,48},{80,64},{96,80},{112,96},{1... | collective-permute-start | bytes 1572872 | tf_op jit(solution)/shard_map/ppermute | solution.py:17
  110.7 11.3 %collective-permute-start.7 = (bf16[1,64,4096]{2,1,0:T(8,128)(2,1)S(1)}, bf16[1,64,4096]{2,1,0:T(8,128)(2,1)S(1)}, u32[]{:S(2)}, u32[]{:S(2)}) collective-permute-start(bf16[1,64,4096]{2,1,0:T(8,128)(2,1)S(1)} %collective-permute-done.6), channel_id=1, source_target_pairs={{0,240},{16,0},{32,16},{48,32},{64,48},{80,64},{96,80},{112,96},{1... | collective-permute-start | bytes 1572872 | tf_op jit(solution)/shard_map/ppermute | solution.py:17
  142.6 128.1 %all-to-all-start = ((bf16[16,54,4096]{2,1,0:T(8,128)(2,1)}), bf16[16,54,4096]{2,1,0:T(8,128)(2,1)}, u32[]{:S(2)}, u32[]{:S(2)}) async-start(bf16[16,54,4096]{2,1,0:T(8,128)(2,1)} %reshape.244), calls=%async_computation | async-start | bytes 14680064 | tf_op jit(solution)/shard_map/all_to_all | solution.py:112
where the time goes:
time: 281 us; the launch traced here: 279 us
  other arithmetic  105 us (37%)
  waiting for transfers between devices  86.5 us (31%)
  starting transfers between devices  45.8 us (16%)
  local copies, waits for them, and re-layouts  37.8 us (13%)
  matrix products  4.28 us (2%)
    convert_element_type x1, other arithmetic, lag_table(): return values.astype(jnp.bfloat16)  71 us
    ppermute x8, waiting for transfers between devices, passed_along(): lax.ppermute(value, axis, [(i, (i + by) % peers) for i in range(peers)])  43.6 us
    all_to_all x1, waiting for transfers between devices, local(): lax.all_to_all(outgoing, 'win', split_axis=0, concat_axis=0, tiled=True)  42.8 us
    ppermute x8, starting transfers between devices, passed_along(): lax.ppermute(value, axis, [(i, (i + by) % peers) for i in range(peers)])  31.6 us
    all_to_all x1, starting transfers between devices, local(): lax.all_to_all(outgoing, 'win', split_axis=0, concat_axis=0, tiled=True)  14.2 us
    scatter x1, local copies, waits for them, and re-layouts, local(): jnp.zeros((groups * capacity, 2 * bin_count), jnp.bfloat16).at[target]  10.9 us
    another operation x15, other arithmetic  10.2 us
    gather x9, local copies, waits for them, and re-layouts, cross_rows(): left_rows = jnp.take(own_block, first_index, axis=1).astype(jnp.float32)  10.1 us
  transfers between devices with their start and end apart: 9, of which 8 were waited for; matrix products, arithmetic and copies ran while one was open for 37% of the time, Pallas kernels for 0%

commit v1 on v0

v1 whole, which is shorter than its diff:
```python
import math

import jax
import jax.numpy as jnp
from jax import lax
from jax.sharding import PartitionSpec as P

LAGS = 1024
SMOOTH_HALF = 10


floor_level = 0.5


def shifted(value, axis, pairs):
    return lax.ppermute(value, axis, pairs)


def whiten(spectra, half_width):
    bin_count = spectra.shape[-1] // 2
    real_part = spectra[..., :bin_count].astype(jnp.float32)
    imag_part = spectra[..., bin_count:].astype(jnp.float32)
    amplitude = jnp.sqrt(real_part * real_part + imag_part * imag_part)
    padded = jnp.pad(amplitude, ((0, 0), (half_width, half_width)))
    running = padded[..., 0:bin_count]
    for offset in range(1, 2 * half_width + 1):
        running = running + padded[..., offset : offset + bin_count]
    smooth = running / (2 * half_width + 1)
    inverse = 1.0 / jnp.maximum(smooth, floor_level)
    return jnp.concatenate([real_part * inverse, imag_part * inverse], axis=-1).astype(jnp.bfloat16)


def cross_rows(own_block, other_block, first_index, second_index):
    bin_count = own_block.shape[-1] // 2
    left_rows = jnp.take(own_block, first_index, axis=0).astype(jnp.float32)
    right_rows = jnp.take(other_block, second_index, axis=0).astype(jnp.float32)
    left_real, left_imag = (left_rows[..., :bin_count], left_rows[..., bin_count:])
    right_real, right_imag = (right_rows[..., :bin_count], right_rows[..., bin_count:])
    real_cross = left_real * right_real + left_imag * right_imag
    imag_cross = left_imag * right_real - left_real * right_imag
    return jnp.concatenate([real_cross, imag_cross], axis=-1).astype(jnp.bfloat16)


def owner_slots(owners, groups):
    flat_owner = owners.reshape(-1)
    owner_hits = (flat_owner[:, None] == jnp.arange(groups, dtype=jnp.int32)[None, :]).astype(
        jnp.int32
    )
    before = jnp.cumsum(owner_hits, axis=0) - owner_hits
    return (flat_owner, jnp.sum(before * owner_hits, axis=1))


def angle_tables(count, step, lag_count):
    period = 2 * 2048
    lag_value = jnp.arange(lag_count, dtype=jnp.int32) - lag_count // 2
    m = jnp.arange(count, dtype=jnp.int32)
    phase = jnp.mod((m * step)[:, None] * lag_value[None, :], period)
    angle = phase.astype(jnp.float32) * (2.0 * math.pi / period)
    return jnp.cos(angle), jnp.sin(angle)


def build_table(bin_count, lag_count):
    hi_step = 64
    hi_count = bin_count // hi_step
    cos_hi, sin_hi = angle_tables(hi_count, hi_step, lag_count)
    cos_lo, sin_lo = angle_tables(hi_step, 1, lag_count)
    cos_full = cos_hi[:, None, :] * cos_lo[None, :, :] - sin_hi[:, None, :] * sin_lo[None, :, :]
    sin_full = sin_hi[:, None, :] * cos_lo[None, :, :] + cos_hi[:, None, :] * sin_lo[None, :, :]
    cos_full = cos_full.reshape(bin_count, lag_count)
    sin_full = sin_full.reshape(bin_count, lag_count)
    frequency = jnp.arange(bin_count, dtype=jnp.int32)
    weight = jnp.where(frequency == 0, 1.0, 2.0).astype(jnp.float32)[:, None]
    return jnp.concatenate([cos_full * weight, -sin_full * weight], axis=0).astype(jnp.bfloat16)


def local(spectra, pair_first, pair_second, pair_owner):
    groups = lax.axis_size("win")
    peers = lax.axis_size("sta")
    bin_count = spectra.shape[-1] // 2
    windows_all = spectra.shape[0] * groups
    factor = 1.0 / math.sqrt(2 * bin_count * windows_all)
    whitened = whiten(spectra[0], SMOOTH_HALF)
    first_rows = pair_first[0]
    second_rows = pair_second[0]
    offsets = first_rows.shape[0]
    me = lax.axis_index("sta")
    is_odd = (me % 2) == 1

    z_pairs = [(i, (i - 2) % peers) for i in range(peers)]
    y_pairs = [(i, i ^ 1) for i in range(peers)]
    rounds = offsets // 2
    chain = [whitened]
    for _ in range(rounds):
        chain.append(shifted(chain[-1], "sta", z_pairs))
    blocks = [None] * offsets
    for r in range(rounds + 1):
        blocks[2 * r] = chain[r]
    for m in range(rounds):
        outgoing_block = jnp.where(is_odd, chain[m], chain[m + 1])
        blocks[2 * m + 1] = shifted(outgoing_block, "sta", y_pairs)

    table = build_table(bin_count, LAGS)
    pieces = []
    for offset_step in range(offsets):
        pieces.append(
            cross_rows(
                whitened, blocks[offset_step], first_rows[offset_step], second_rows[offset_step]
            )
        )
    partial_value = jnp.concatenate(pieces, axis=0)
    transformed = (
        jnp.dot(partial_value, table, preferred_element_type=jnp.float32) * factor
    ).astype(jnp.bfloat16)
    pair_rows = partial_value.shape[0]
    capacity = 2 * pair_rows // groups
    owners, slot_of = owner_slots(pair_owner[0], groups)
    target = owners * capacity + slot_of
    placement = (
        target[None, :] == jnp.arange(groups * capacity, dtype=jnp.int32)[:, None]
    ).astype(jnp.bfloat16)
    outgoing = jnp.dot(placement, transformed, preferred_element_type=jnp.float32).astype(
        jnp.bfloat16
    )
    outgoing = outgoing.reshape(groups, capacity, LAGS)
    received = lax.all_to_all(outgoing, "win", split_axis=0, concat_axis=0, tiled=True)
    result = jnp.sum(received.astype(jnp.float32), axis=0).astype(jnp.bfloat16)
    return result[None]


def solution(mesh):
    placed = (
        P("win", "sta", None),
        P("sta", None, None),
        P("sta", None, None),
        P("sta", None, None),
    )
    return jax.shard_map(
        local, mesh=mesh, in_specs=placed, out_specs=P("sta", "win", None), check_vma=False
    )
```

time: 281 us -> 194 us (0.69)
  other arithmetic: 105 us -> 59.3 us
  waiting for transfers between devices: 86.5 us -> 46 us
  blocking collectives: 0 us -> 36.9 us
  starting transfers between devices: 45.8 us -> 15.2 us
  local copies, waits for them, and re-layouts: 37.8 us -> 27.2 us
  matrix products: 4.28 us -> 8.3 us
    convert_element_type x15 -> x16, other arithmetic: 80.5 us -> 15.2 us  [the longest x9 9.37 us: cross_rows(): left_rows = jnp.take(own_block, first_index, axis=0).astype(jnp.float32)]
    all_to_all x1 -> x0, waiting for transfers between devices: 42.8 us -> none  [local(): lax.all_to_all(outgoing, 'win', split_axis=0, concat_axis=0, tiled=True)]
    all_to_all x0 -> x1, blocking collectives: none -> 36.9 us  [local(): lax.all_to_all(outgoing, 'win', split_axis=0, concat_axis=0, tiled=True)]
    ppermute x8, starting transfers between devices: 31.6 us -> 15.2 us  [shifted(): return lax.ppermute(value, axis, pairs)]
    all_to_all x1 -> x0, starting transfers between devices: 14.2 us -> none  [local(): lax.all_to_all(outgoing, 'win', split_axis=0, concat_axis=0, tiled=True)]
    scatter x1 -> x0, local copies, waits for them, and re-layouts: 10.9 us -> none  [local(): jnp.zeros((groups * capacity, 2 * bin_count), jnp.bfloat16).at[target]]
    another operation x15 -> x16, other arithmetic: 10.2 us -> 20.9 us
    reshape x1, local copies, waits for them, and re-layouts: 7.05 us -> 1.68 us  [local(): outgoing = outgoing.reshape(groups, capacity, LAGS)]
  transfers between devices with their start and end apart: 9 -> 8, of which waited for: 8 -> 7; matrix products, arithmetic and copies ran while one was open for 37% -> 34% of each run, Pallas kernels for 0% -> 0%
where the time goes in v1:
time: 194 us; the launch traced here: 193 us
  other arithmetic  59.3 us (31%)
  waiting for transfers between devices  46 us (24%)
  blocking collectives  36.9 us (19%)
  local copies, waits for them, and re-layouts  27.2 us (14%)
  starting transfers between devices  15.2 us (8%)
  matrix products  8.3 us (4%)
    ppermute x8, waiting for transfers between devices, shifted(): return lax.ppermute(value, axis, pairs)  46 us
    all_to_all x1, blocking collectives, local(): lax.all_to_all(outgoing, 'win', split_axis=0, concat_axis=0, tiled=True)  36.9 us
    another operation x16, other arithmetic  20.9 us
    ppermute x8, starting transfers between devices, shifted(): return lax.ppermute(value, axis, pairs)  15.2 us
    gather x9, local copies, waits for them, and re-layouts, cross_rows(): left_rows = jnp.take(own_block, first_index, axis=0).astype(jnp.float32)  12.4 us
    gather x9, local copies, waits for them, and re-layouts, cross_rows(): right_rows = jnp.take(other_block, second_index, axis=0).astype(jnp.float32)  12.3 us
    convert_element_type x9, other arithmetic, cross_rows(): left_rows = jnp.take(own_block, first_index, axis=0).astype(jnp.float32)  9.37 us
    unnamed x9, other arithmetic  6.28 us
  transfers between devices with their start and end apart: 8, of which 7 were waited for; matrix products, arithmetic and copies ran while one was open for 34% of the time, Pallas kernels for 0%

profile of v1, /device:TPU:1, one launch (start us, length us, event | category | flops | bytes accessed | tf_op | source)
XLA Modules:
  0.0 193.5 jit_solution(8146437561502041242)
XLA Ops:
  0.0 1.3 fusion.12
  1.3 3.7 %fusion.13 = (bf16[64,2048]{1,0:T(8,128)(2,1)S(1)}, f32[64,2048]{1,0:T(8,128)S(1)}) fusion(bf16[64,4096]{1,0:T(8,128)(2,1)} %bitcast.79, f32[64,2048]{1,0:T(8,128)S(1)} %fusion.12), kind=kLoop, calls=%fused_computation.39 | loop fusion | flops 3407872 | bytes 1572864 | tf_op jit(solution)/shard_map/convert.24
  5.0 1.0 fusion.14
  6.0 6.5 %collective-permute-start = (bf16[64,4096]{1,0:T(8,128)(2,1)S(1)}, bf16[64,4096]{1,0:T(8,128)(2,1)S(1)}, u32[]{:S(2)}, u32[]{:S(2)}) collective-permute-start(bf16[64,4096]{1,0:T(8,128)(2,1)S(1)} %pad_maximum_fusion), channel_id=1, source_target_pairs={{0,224},{16,240},{32,0},{48,16},{64,32},{80,48},{96,64},{112,80},{... | collective-permute-start | bytes 1572872 | tf_op jit(solution)/shard_map/ppermute | solution.py:16
  14.7 0.8 gather_fusion
  15.4 0.8 gather_fusion.1
  16.2 1.5 gather_fusion.4
  18.4 1.5 gather_fusion.6
  19.9 1.6 gather_fusion.8
  23.2 1.6 gather_fusion.10
  24.8 1.5 gather_fusion.12
  26.9 1.6 gather_fusion.14
  28.5 1.5 gather_fusion.16
  30.1 1.8 fusion.33
  31.8 1.3 fusion.35
  33.2 1.2 reduce-window.6
  35.3 1.1 select_convert_fusion.15
  36.4 0.8 select_convert_fusion.17
  37.2 0.8 select_convert_fusion.16
  38.2 1.2 select_convert_fusion.13
  39.5 2.0 %select_convert_fusion.11 = f32[48,4096]{1,0:T(8,128)} fusion(bf16[48,4096]{1,0:T(8,128)(2,1)} %gather_fusion.6, pred[48]{0:T(512)(128)(4,1)} %get-tuple-element.78), kind=kLoop, calls=%fused_computation.84 | loop fusion | flops 393216 | bytes 1179696 | tf_op jit(solution)/shard_map/convert_element_type | solution.py:35
  41.5 1.0 select_convert_fusion.9
  42.7 1.0 select_convert_fusion.5
  43.7 1.0 select_convert_fusion.3
  44.8 1.0 select_convert_fusion.1
  45.8 2.5 %multiply_subtract_fusion = (f32[32,64,1024]{2,1,0:T(8,128)S(1)}, f32[32,64,1024]{2,1,0:T(8,128)S(1)}) fusion(f32[64,1024]{1,0:T(8,128)S(1)} %copy-done.10, f32[32,1024]{1,0:T(8,128)S(1)} %copy-done.23, f32[64,1024]{1,0:T(8,128)S(1)} %get-tuple-element.104, f32[32,1024]{1,0:T(8,128)S(1)} %get-tuple-element.70), kind=kLoop, calls=%fused_computation.27 | loop fusion | flops 14680064 | bytes 17563648 | tf_op jit(solution)/shard_map/sub | solution.py:67
  48.3 4.9 %fusion.5 = (bf16[2048,1024]{1,0:T(8,128)(2,1)}, bf16[2048,1024]{1,0:T(8,128)(2,1)}) fusion(f32[32,64,1024]{2,1,0:T(8,128)S(1)} %get-tuple-element.62, f32[2048]{0:T(1024)S(1)} %fusion.38, f32[32,64,1024]{2,1,0:T(8,128)S(1)} %get-tuple-element.63), kind=kLoop, calls=%fused_computation.25 | loop fusion | flops 8388608 | bytes 25174016 | tf_op jit(solution)/shard_map/convert.4
  53.3 0.8 maximum_dynamic-update-slice_fusion.8
  54.8 1.7 gather_fusion.5
  56.5 1.1 select_convert_fusion.12
  57.6 0.9 add_convert_fusion.6
  58.4 8.2 %collective-permute-done.2 = bf16[64,4096]{1,0:T(8,128)(2,1)S(1)} collective-permute-done((bf16[64,4096]{1,0:T(8,128)(2,1)S(1)}, bf16[64,4096]{1,0:T(8,128)(2,1)S(1)}, u32[]{:S(2)}, u32[]{:S(2)}) %collective-permute-start.2) | collective-permute-done | bytes 524320 | tf_op jit(solution)/shard_map/ppermute | solution.py:16
  66.6 1.9 %collective-permute-start.4 = (bf16[64,4096]{1,0:T(8,128)(2,1)S(1)}, bf16[64,4096]{1,0:T(8,128)(2,1)S(1)}, u32[]{:S(2)}, u32[]{:S(2)}) collective-permute-start(bf16[64,4096]{1,0:T(8,128)(2,1)S(1)} %collective-permute-done.2), channel_id=1, source_target_pairs={{0,224},{16,240},{32,0},{48,16},{64,32},{80,48},{96,64},{112,80},{... | collective-permute-start | bytes 1572872 | tf_op jit(solution)/shard_map/ppermute | solution.py:16
  68.5 0.9 gather_fusion.9
  69.6 2.0 %add_convert_fusion.4 = (bf16[48,2048]{1,0:T(8,128)(2,1)}, bf16[48,2048]{1,0:T(8,128)(2,1)}) fusion(f32[48,4096]{1,0:T(8,128)S(1)} %select_convert_fusion.8, f32[48,4096]{1,0:T(8,128)} %select_convert_fusion.9), kind=kLoop, calls=%fused_computation.103 | loop fusion | flops 786432 | bytes 1966080 | tf_op jit(solution)/shard_map/convert.14
  71.6 6.7 %collective-permute-done.4 = bf16[64,4096]{1,0:T(8,128)(2,1)S(1)} collective-permute-done((bf16[64,4096]{1,0:T(8,128)(2,1)S(1)}, bf16[64,4096]{1,0:T(8,128)(2,1)S(1)}, u32[]{:S(2)}, u32[]{:S(2)}) %collective-permute-start.4) | collective-permute-done | bytes 524320 | tf_op jit(solution)/shard_map/ppermute | solution.py:16
  78.3 3.1 %collective-permute-start.6 = (bf16[64,4096]{1,0:T(8,128)(2,1)S(1)}, bf16[64,4096]{1,0:T(8,128)(2,1)S(1)}, u32[]{:S(2)}, u32[]{:S(2)}) collective-permute-start(bf16[64,4096]{1,0:T(8,128)(2,1)S(1)} %collective-permute-done.4), channel_id=1, source_target_pairs={{0,224},{16,240},{32,0},{48,16},{64,32},{80,48},{96,64},{112,80},{... | collective-permute-start | bytes 1572872 | tf_op jit(solution)/shard_map/ppermute | solution.py:16
  81.4 1.6 gather_fusion.13
  83.1 1.1 select_convert_fusion.4
  84.2 2.0 %add_convert_fusion.2 = (bf16[48,2048]{1,0:T(8,128)(2,1)}, bf16[48,2048]{1,0:T(8,128)(2,1)}) fusion(f32[48,4096]{1,0:T(8,128)S(1)} %select_convert_fusion.4, f32[48,4096]{1,0:T(8,128)} %select_convert_fusion.5), kind=kLoop, calls=%fused_computation.99 | loop fusion | flops 786432 | bytes 1966080 | tf_op jit(solution)/shard_map/convert.10
  86.2 3.9 %collective-permute-done.6 = bf16[64,4096]{1,0:T(8,128)(2,1)S(1)} collective-permute-done((bf16[64,4096]{1,0:T(8,128)(2,1)S(1)}, bf16[64,4096]{1,0:T(8,128)(2,1)S(1)}, u32[]{:S(2)}, u32[]{:S(2)}) %collective-permute-start.6) | collective-permute-done | bytes 524320 | tf_op jit(solution)/shard_map/ppermute | solution.py:16
  90.0 1.9 broadcast_select_fusion
  91.9 1.3 collective-permute-start.1
  93.4 1.3 collective-permute-start.5
  94.9 1.6 gather_fusion.17
  96.4 1.1 select_convert_fusion
  97.6 2.0 %add_convert_fusion = (bf16[48,2048]{1,0:T(8,128)(2,1)}, bf16[48,2048]{1,0:T(8,128)(2,1)}) fusion(f32[48,4096]{1,0:T(8,128)S(1)} %select_convert_fusion, f32[48,4096]{1,0:T(8,128)} %select_convert_fusion.1), kind=kLoop, calls=%fused_computation.95 | loop fusion | flops 786432 | bytes 1966080 | tf_op jit(solution)/shard_map/convert.6
  99.5 2.6 %collective-permute-done.1 = bf16[64,4096]{1,0:T(8,128)(2,1)S(1)} collective-permute-done((bf16[64,4096]{1,0:T(8,128)(2,1)}, bf16[64,4096]{1,0:T(8,128)(2,1)S(1)}, u32[]{:S(2)}, u32[]{:S(2)}) %collective-permute-start.1) | collective-permute-done | bytes 524320 | tf_op jit(solution)/shard_map/ppermute | solution.py:16
  102.1 1.5 gather_fusion.3
  103.7 9.7 %collective-permute-done.3 = bf16[64,4096]{1,0:T(8,128)(2,1)S(1)} collective-permute-done((bf16[64,4096]{1,0:T(8,128)(2,1)}, bf16[64,4096]{1,0:T(8,128)(2,1)S(1)}, u32[]{:S(2)}, u32[]{:S(2)}) %collective-permute-start.3) | collective-permute-done | bytes 524320 | tf_op jit(solution)/shard_map/ppermute | solution.py:16
  113.3 1.6 gather_fusion.7
  114.9 1.4 select_convert_fusion.10
  116.3 2.0 %add_convert_fusion.7 = (bf16[48,2048]{1,0:T(8,128)(2,1)}, bf16[48,2048]{1,0:T(8,128)(2,1)}) fusion(f32[48,4096]{1,0:T(8,128)S(1)} %get-tuple-element.109, f32[48,4096]{1,0:T(8,128)} %select_convert_fusion.15), kind=kLoop, calls=%fused_computation.109 | loop fusion | flops 786432 | bytes 1966080 | tf_op jit(solution)/shard_map/convert.20
  118.3 6.3 %collective-permute-done.5 = bf16[64,4096]{1,0:T(8,128)(2,1)S(1)} collective-permute-done((bf16[64,4096]{1,0:T(8,128)(2,1)}, bf16[64,4096]{1,0:T(8,128)(2,1)S(1)}, u32[]{:S(2)}, u32[]{:S(2)}) %collective-permute-start.5) | collective-permute-done | bytes 524320 | tf_op jit(solution)/shard_map/ppermute | solution.py:16
  124.6 1.7 gather_fusion.11
  126.3 0.9 add_convert_fusion.5
  127.1 8.7 %collective-permute-done.7 = bf16[64,4096]{1,0:T(8,128)(2,1)S(1)} collective-permute-done((bf16[64,4096]{1,0:T(8,128)(2,1)}, bf16[64,4096]{1,0:T(8,128)(2,1)S(1)}, u32[]{:S(2)}, u32[]{:S(2)}) %collective-permute-start.7) | collective-permute-done | bytes 524320 | tf_op jit(solution)/shard_map/ppermute | solution.py:16
  135.8 0.9 gather_fusion.15
  139.3 0.8 maximum_dynamic-update-slice_fusion.5
  144.0 6.0 %multiply_convert_fusion = bf16[432,1024]{1,0:T(8,128)(2,1)S(1)} fusion(bf16[432,4096]{1,0:T(8,128)(2,1)} %maximum_dynamic-update-slice_fusion, bf16[2048,1024]{1,0:T(8,128)(2,1)S(1)} %copy-done.1, bf16[2048,1024]{1,0:T(8,128)(2,1)S(1)} %copy-done), kind=kOutput, calls=%fused_computation.28 | convolution fusion | flops 3641540608 | bytes 12812288 | tf_op jit(solution)/shard_map/dot_general | solution.py:112
  150.0 2.3 %fusion.7 = bf16[864,1024]{1,0:T(8,128)(2,1)} fusion(bf16[432,1024]{1,0:T(8,128)(2,1)S(1)} %multiply_convert_fusion, s32[432]{0:T(512)S(1)} %copy-done.37), kind=kOutput, calls=%fused_computation.31 | convolution fusion | flops 765669888 | bytes 2655936 | tf_op jit(solution)/shard_map/dot_general | solution.py:121
  152.3 1.7 reshape.209
  154.0 36.9 %all_to_all.5 = bf16[16,54,1024]{2,1,0:T(8,128)(2,1)} all-to-all(bf16[16,54,1024]{2,1,0:T(8,128)(2,1)S(1)} %reshape.209), channel_id=1, replica_groups=mesh['sta'=16,'win'=16] {'win'}, dimensions={0} | all-to-all | bytes 3538944 | tf_op jit(solution)/shard_map/all_to_all | solution.py:125
  191.0 2.5 %reduce_sum.22 = bf16[54,1024]{1,0:T(8,128)(2,1)} reduce(bf16[16,54,1024]{2,1,0:T(8,128)(2,1)} %all_to_all.5, bf16[]{:T(256)} %constant.85.clone.1), dimensions={0}, to_apply=%region_3.5 | reduce | flops 829440 | bytes 1880066 | tf_op jit(solution)/shard_map/reduce_sum | solution.py:126
  (131 shorter events, 14.0 us)
Async XLA Ops:
  0.0 12.5 %copy-start.24 = (s32[1,9,48]{2,0,1:T(1,128)S(1)}, s32[1,9,48]{2,0,1:T(1,128)}, u32[]{:S(2)}) copy-start(s32[1,9,48]{2,0,1:T(1,128)} %param.8) | copy-start | bytes 5188
  0.0 13.2 %copy-start.25 = (s32[1,9,48]{2,0,1:T(1,128)S(1)}, s32[1,9,48]{2,0,1:T(1,128)}, u32[]{:S(2)}) copy-start(s32[1,9,48]{2,0,1:T(1,128)} %param.7) | copy-start | bytes 5188
  6.0 48.0 %collective-permute-start = (bf16[64,4096]{1,0:T(8,128)(2,1)S(1)}, bf16[64,4096]{1,0:T(8,128)(2,1)S(1)}, u32[]{:S(2)}, u32[]{:S(2)}) collective-permute-start(bf16[64,4096]{1,0:T(8,128)(2,1)S(1)} %pad_maximum_fusion), channel_id=1, source_target_pairs={{0,224},{16,240},{32,0},{48,16},{64,32},{80,48},{96,64},{112,80},{... | collective-permute-start | bytes 1572872 | tf_op jit(solution)/shard_map/ppermute | solution.py:16
  26.9 6.1 %copy-start.26 = (s32[1,9,48]{2,0,1:T(1,128)S(1)}, s32[1,9,48]{2,0,1:T(1,128)}, u32[]{:S(2)}) copy-start(s32[1,9,48]{2,0,1:T(1,128)} %param.9) | copy-start | bytes 5188
  36.4 5.1 %copy-start.4 = (bf16[48,4096]{1,0:T(8,128)(2,1)S(1)}, bf16[48,4096]{1,0:T(8,128)(2,1)}, u32[]{:S(2)}) copy-start(bf16[48,4096]{1,0:T(8,128)(2,1)} %gather_fusion.8) | copy-start | bytes 1179652
  36.4 5.1 %copy-start.35 = (pred[48]{0:T(512)(128)(4,1)S(1)}, pred[48]{0:T(512)(128)(4,1)}, u32[]{:S(2)}) copy-start(pred[48]{0:T(512)(128)(4,1)} %get-tuple-element.76) | copy-start | bytes 148
  37.2 5.4 %copy-start.5 = (bf16[48,4096]{1,0:T(8,128)(2,1)S(1)}, bf16[48,4096]{1,0:T(8,128)(2,1)}, u32[]{:S(2)}) copy-start(bf16[48,4096]{1,0:T(8,128)(2,1)} %gather_fusion.10) | copy-start | bytes 1179652
  37.2 5.3 %copy-start.34 = (pred[48]{0:T(512)(128)(4,1)S(1)}, pred[48]{0:T(512)(128)(4,1)}, u32[]{:S(2)}) copy-start(pred[48]{0:T(512)(128)(4,1)} %get-tuple-element.74) | copy-start | bytes 148
  38.1 4.6 %copy-start.6 = (bf16[48,4096]{1,0:T(8,128)(2,1)S(1)}, bf16[48,4096]{1,0:T(8,128)(2,1)}, u32[]{:S(2)}) copy-start(bf16[48,4096]{1,0:T(8,128)(2,1)} %gather_fusion.12) | copy-start | bytes 1179652
  38.1 4.6 %copy-start.33 = (pred[48]{0:T(512)(128)(4,1)S(1)}, pred[48]{0:T(512)(128)(4,1)}, u32[]{:S(2)}) copy-start(pred[48]{0:T(512)(128)(4,1)} %get-tuple-element.72) | copy-start | bytes 148
  38.1 5.7 %copy-start.8 = (bf16[48,4096]{1,0:T(8,128)(2,1)S(1)}, bf16[48,4096]{1,0:T(8,128)(2,1)}, u32[]{:S(2)}) copy-start(bf16[48,4096]{1,0:T(8,128)(2,1)} %gather_fusion.14) | copy-start | bytes 1179652
  38.1 5.6 %copy-start.32 = (pred[48]{0:T(512)(128)(4,1)S(1)}, pred[48]{0:T(512)(128)(4,1)}, u32[]{:S(2)}) copy-start(pred[48]{0:T(512)(128)(4,1)} %get-tuple-element.86) | copy-start | bytes 148
  38.2 6.6 %copy-start.7 = (bf16[48,4096]{1,0:T(8,128)(2,1)S(1)}, bf16[48,4096]{1,0:T(8,128)(2,1)}, u32[]{:S(2)}) copy-start(bf16[48,4096]{1,0:T(8,128)(2,1)} %gather_fusion.16) | copy-start | bytes 1179652
  38.2 6.6 %copy-start.31 = (pred[48]{0:T(512)(128)(4,1)S(1)}, pred[48]{0:T(512)(128)(4,1)}, u32[]{:S(2)}) copy-start(pred[48]{0:T(512)(128)(4,1)} %get-tuple-element.6) | copy-start | bytes 148
  39.4 6.4 %copy-start.10 = (f32[64,1024]{1,0:T(8,128)S(1)}, f32[64,1024]{1,0:T(8,128)}, u32[]{:S(2)}) copy-start(f32[64,1024]{1,0:T(8,128)} %get-tuple-element.105) | copy-start | bytes 786436
  39.5 6.4 %copy-start.23 = (f32[32,1024]{1,0:T(8,128)S(1)}, f32[32,1024]{1,0:T(8,128)}, u32[]{:S(2)}) copy-start(f32[32,1024]{1,0:T(8,128)} %get-tuple-element.71) | copy-start | bytes 393220
  48.3 5.0 %copy-start.36 = (s32[48]{0:T(128)S(1)}, s32[48]{0:T(128)}, u32[]{:S(2)}) copy-start(s32[48]{0:T(128)} %get-tuple-element.9) | copy-start | bytes 580
  53.2 3.2 %copy-start.30 = (pred[48]{0:T(512)(128)(4,1)S(1)}, pred[48]{0:T(512)(128)(4,1)}, u32[]{:S(2)}) copy-start(pred[48]{0:T(512)(128)(4,1)} %get-tuple-element.96) | copy-start | bytes 148
  54.1 12.5 %collective-permute-start.2 = (bf16[64,4096]{1,0:T(8,128)(2,1)S(1)}, bf16[64,4096]{1,0:T(8,128)(2,1)S(1)}, u32[]{:S(2)}, u32[]{:S(2)}) collective-permute-start(bf16[64,4096]{1,0:T(8,128)(2,1)S(1)} %collective-permute-done), channel_id=1, source_target_pairs={{0,224},{16,240},{32,0},{48,16},{64,32},{80,48},{96,64},{112,80},{... | collective-permute-start | bytes 1572872 | tf_op jit(solution)/shard_map/ppermute | solution.py:16
  56.4 13.0 %copy-start.29 = (pred[48]{0:T(512)(128)(4,1)S(1)}, pred[48]{0:T(512)(128)(4,1)}, u32[]{:S(2)}) copy-start(pred[48]{0:T(512)(128)(4,1)} %get-tuple-element.92) | copy-start | bytes 148
  66.6 11.7 %collective-permute-start.4 = (bf16[64,4096]{1,0:T(8,128)(2,1)S(1)}, bf16[64,4096]{1,0:T(8,128)(2,1)S(1)}, u32[]{:S(2)}, u32[]{:S(2)}) collective-permute-start(bf16[64,4096]{1,0:T(8,128)(2,1)S(1)} %collective-permute-done.2), channel_id=1, source_target_pairs={{0,224},{16,240},{32,0},{48,16},{64,32},{80,48},{96,64},{112,80},{... | collective-permute-start | bytes 1572872 | tf_op jit(solution)/shard_map/ppermute | solution.py:16
  69.4 13.6 %copy-start.28 = (pred[48]{0:T(512)(128)(4,1)S(1)}, pred[48]{0:T(512)(128)(4,1)}, u32[]{:S(2)}) copy-start(pred[48]{0:T(512)(128)(4,1)} %get-tuple-element.88) | copy-start | bytes 148
  78.3 11.8 %collective-permute-start.6 = (bf16[64,4096]{1,0:T(8,128)(2,1)S(1)}, bf16[64,4096]{1,0:T(8,128)(2,1)S(1)}, u32[]{:S(2)}, u32[]{:S(2)}) collective-permute-start(bf16[64,4096]{1,0:T(8,128)(2,1)S(1)} %collective-permute-done.4), channel_id=1, source_target_pairs={{0,224},{16,240},{32,0},{48,16},{64,32},{80,48},{96,64},{112,80},{... | collective-permute-start | bytes 1572872 | tf_op jit(solution)/shard_map/ppermute | solution.py:16
  86.2 10.3 %copy-start.27 = (pred[48]{0:T(512)(128)(4,1)S(1)}, pred[48]{0:T(512)(128)(4,1)}, u32[]{:S(2)}) copy-start(pred[48]{0:T(512)(128)(4,1)} %get-tuple-element.8) | copy-start | bytes 148
  91.9 10.2 %collective-permute-start.1 = (bf16[64,4096]{1,0:T(8,128)(2,1)}, bf16[64,4096]{1,0:T(8,128)(2,1)S(1)}, u32[]{:S(2)}, u32[]{:S(2)}) collective-permute-start(bf16[64,4096]{1,0:T(8,128)(2,1)} %get-tuple-element.67), channel_id=1, source_target_pairs={{0,16},{16,0},{32,48},{48,32},{64,80},{80,64},{96,112},{112,96},{1... | collective-permute-start | bytes 1572872 | tf_op jit(solution)/shard_map/ppermute | solution.py:16
  93.2 20.1 %collective-permute-start.3 = (bf16[64,4096]{1,0:T(8,128)(2,1)}, bf16[64,4096]{1,0:T(8,128)(2,1)S(1)}, u32[]{:S(2)}, u32[]{:S(2)}) collective-permute-start(bf16[64,4096]{1,0:T(8,128)(2,1)} %get-tuple-element.66), channel_id=1, source_target_pairs={{0,16},{16,0},{32,48},{48,32},{64,80},{80,64},{96,112},{112,96},{1... | collective-permute-start | bytes 1572872 | tf_op jit(solution)/shard_map/ppermute | solution.py:16
  93.4 31.2 %collective-permute-start.5 = (bf16[64,4096]{1,0:T(8,128)(2,1)}, bf16[64,4096]{1,0:T(8,128)(2,1)S(1)}, u32[]{:S(2)}, u32[]{:S(2)}) collective-permute-start(bf16[64,4096]{1,0:T(8,128)(2,1)} %get-tuple-element.65), channel_id=1, source_target_pairs={{0,16},{16,0},{32,48},{48,32},{64,80},{80,64},{96,112},{112,96},{1... | collective-permute-start | bytes 1572872 | tf_op jit(solution)/shard_map/ppermute | solution.py:16
  94.7 41.1 %collective-permute-start.7 = (bf16[64,4096]{1,0:T(8,128)(2,1)}, bf16[64,4096]{1,0:T(8,128)(2,1)S(1)}, u32[]{:S(2)}, u32[]{:S(2)}) collective-permute-start(bf16[64,4096]{1,0:T(8,128)(2,1)} %get-tuple-element.64), channel_id=1, source_target_pairs={{0,16},{16,0},{32,48},{48,32},{64,80},{80,64},{96,112},{112,96},{1... | collective-permute-start | bytes 1572872 | tf_op jit(solution)/shard_map/ppermute | solution.py:16
  99.5 15.4 %copy-start.40 = (pred[48]{0:T(512)(128)(4,1)S(1)}, pred[48]{0:T(512)(128)(4,1)}, u32[]{:S(2)}) copy-start(pred[48]{0:T(512)(128)(4,1)} %get-tuple-element.94) | copy-start | bytes 148
  99.5 15.4 %copy-start.41 = (pred[48]{0:T(512)(128)(4,1)S(1)}, pred[48]{0:T(512)(128)(4,1)}, u32[]{:S(2)}) copy-start(pred[48]{0:T(512)(128)(4,1)} %get-tuple-element.98) | copy-start | bytes 148
  114.9 11.4 %copy-start.3 = (f32[48,4096]{1,0:T(8,128)S(1)}, f32[48,4096]{1,0:T(8,128)}, u32[]{:S(2)}) copy-start(f32[48,4096]{1,0:T(8,128)} %select_convert_fusion.11) | copy-start | bytes 2359300
  126.3 10.5 %copy-start.38 = (pred[48]{0:T(512)(128)(4,1)S(1)}, pred[48]{0:T(512)(128)(4,1)}, u32[]{:S(2)}) copy-start(pred[48]{0:T(512)(128)(4,1)} %get-tuple-element.90) | copy-start | bytes 148
  126.3 10.5 %copy-start.39 = (pred[48]{0:T(512)(128)(4,1)S(1)}, pred[48]{0:T(512)(128)(4,1)}, u32[]{:S(2)}) copy-start(pred[48]{0:T(512)(128)(4,1)} %get-tuple-element.102) | copy-start | bytes 148
  127.1 9.6 %copy-start.9 = (bf16[48,4096]{1,0:T(8,128)(2,1)S(1)}, bf16[48,4096]{1,0:T(8,128)(2,1)}, u32[]{:S(2)}) copy-start(bf16[48,4096]{1,0:T(8,128)(2,1)} %gather_fusion.11) | copy-start | bytes 1179652
  127.1 10.0 %copy-start.2 = (f32[48,4096]{1,0:T(8,128)S(1)}, f32[48,4096]{1,0:T(8,128)}, u32[]{:S(2)}) copy-start(f32[48,4096]{1,0:T(8,128)} %select_convert_fusion.3) | copy-start | bytes 2359300
  136.7 0.9 copy-start.19
  136.7 1.0 copy-start.20
  136.8 1.8 copy-start.11
  136.8 1.7 copy-start.12
  136.8 2.5 %copy-start.21 = (bf16[48,2048]{1,0:T(8,128)(2,1)S(1)}, bf16[48,2048]{1,0:T(8,128)(2,1)}, u32[]{:S(2)}) copy-start(bf16[48,2048]{1,0:T(8,128)(2,1)} %get-tuple-element.54) | copy-start | bytes 589828
  136.8 2.5 %copy-start.22 = (bf16[48,2048]{1,0:T(8,128)(2,1)S(1)}, bf16[48,2048]{1,0:T(8,128)(2,1)}, u32[]{:S(2)}) copy-start(bf16[48,2048]{1,0:T(8,128)(2,1)} %get-tuple-element.55) | copy-start | bytes 589828
  137.0 3.1 %copy-start.13 = (bf16[48,2048]{1,0:T(8,128)(2,1)S(1)}, bf16[48,2048]{1,0:T(8,128)(2,1)}, u32[]{:S(2)}) copy-start(bf16[48,2048]{1,0:T(8,128)(2,1)} %get-tuple-element.52) | copy-start | bytes 589828
  137.0 3.1 %copy-start.14 = (bf16[48,2048]{1,0:T(8,128)(2,1)S(1)}, bf16[48,2048]{1,0:T(8,128)(2,1)}, u32[]{:S(2)}) copy-start(bf16[48,2048]{1,0:T(8,128)(2,1)} %get-tuple-element.53) | copy-start | bytes 589828
  137.0 4.7 %copy-start.15 = (bf16[48,2048]{1,0:T(8,128)(2,1)S(1)}, bf16[48,2048]{1,0:T(8,128)(2,1)}, u32[]{:S(2)}) copy-start(bf16[48,2048]{1,0:T(8,128)(2,1)} %get-tuple-element.48) | copy-start | bytes 589828
  137.0 4.7 %copy-start.16 = (bf16[48,2048]{1,0:T(8,128)(2,1)S(1)}, bf16[48,2048]{1,0:T(8,128)(2,1)}, u32[]{:S(2)}) copy-start(bf16[48,2048]{1,0:T(8,128)(2,1)} %get-tuple-element.49) | copy-start | bytes 589828
  137.0 7.0 %copy-start.1 = (bf16[2048,1024]{1,0:T(8,128)(2,1)S(1)}, bf16[2048,1024]{1,0:T(8,128)(2,1)}, u32[]{:S(2)}) copy-start(bf16[2048,1024]{1,0:T(8,128)(2,1)} %get-tuple-element.69) | copy-start | bytes 12582916
  137.2 6.0 %copy-start.17 = (bf16[48,2048]{1,0:T(8,128)(2,1)S(1)}, bf16[48,2048]{1,0:T(8,128)(2,1)}, u32[]{:S(2)}) copy-start(bf16[48,2048]{1,0:T(8,128)(2,1)} %get-tuple-element.44) | copy-start | bytes 589828
  137.2 6.0 %copy-start.18 = (bf16[48,2048]{1,0:T(8,128)(2,1)S(1)}, bf16[48,2048]{1,0:T(8,128)(2,1)}, u32[]{:S(2)}) copy-start(bf16[48,2048]{1,0:T(8,128)(2,1)} %get-tuple-element.45) | copy-start | bytes 589828
  137.3 6.7 %copy-start = (bf16[2048,1024]{1,0:T(8,128)(2,1)S(1)}, bf16[2048,1024]{1,0:T(8,128)(2,1)}, u32[]{:S(2)}) copy-start(bf16[2048,1024]{1,0:T(8,128)(2,1)} %get-tuple-element.68) | copy-start | bytes 12582916
  144.0 6.0 %copy-start.37 = (s32[432]{0:T(512)S(1)}, s32[432]{0:T(512)}, u32[]{:S(2)}) copy-start(s32[432]{0:T(512)} %multiply_add_fusion) | copy-start | bytes 5188
